TPU v7x, 256 devices: a whole 4x4x8 slice. The times are simulated.
256 devices in a mesh: dp: 8 (over y_hi, x), seq: 16 (over y_lo, z), segment: 2 (over core).
Axes of the slice: x: 4, y: 4 (y_hi: 2, y_lo: 2; y = y_hi * 2 + y_lo), z: 8, core: 2. Of those that a mesh axis runs over, the one named last changes fastest.
Arguments:
- saved_input: bfloat16 [2, 8, 8192, 256], P('segment', 'dp', 'seq'), may hold values from -6 to 6
- upstream: bfloat16 [8, 8192, 256], P('dp', 'seq'), may hold values from -6 to 6
- clip_lengths: int32 [8, 32], P('dp'), may hold values from 1 to 2048, 8192 in all within a row
- conv_a: bfloat16 [2, 3, 7, 256, 256], P('segment'), may hold values from -0.125 to 0.125
- bias_a: float32 [2, 3, 256], P('segment'), may hold values from -3 to 3
- conv_b: bfloat16 [2, 3, 256, 256], P('segment'), may hold values from -0.375 to 0.375
Outputs:
- section_input_grad: bfloat16 [2, 8, 8192, 256], P('segment', 'dp', 'seq')
- grad_conv_a: float32 [2, 3, 7, 256, 256], P('segment')
- grad_bias_a: float32 [2, 3, 256], P('segment')
- grad_conv_b: float32 [2, 3, 256, 256], P('segment')
Inputs may be any that keep to these rules, and one draw needn't show every extreme that they name: `clip_lengths`: each row's 32 lengths sum to 8192, and the longest is exactly 2048.
All inputs are finite; a program needn't handle non-finite values.
Results may differ from a plain program's by a relative error of at most 0.02.
Values may be sent and summed in bfloat16 or wider, within the bound.
No kernel may reach another device: no remote copies, remote signals or barrier semaphores. Data moves between devices by JAX's collectives and lax.ppermute only.
A program may use at most 128 MiB of HBM per device.

v0:
```python
import jax
import jax.numpy as jnp
from jax import lax
from jax.sharding import PartitionSpec as P

KERNEL = 7
UNITS = 3


def with_halo(cells, sides, width):
    for axis, dim in sides:
        count = lax.axis_size(axis)
        ends = count - 1
        head = lax.slice_in_dim(cells, 0, width, axis=dim)
        tail = lax.slice_in_dim(cells, cells.shape[dim] - width, cells.shape[dim], axis=dim)
        cells = jnp.concatenate(
            [
                lax.ppermute(tail, axis, [(i, (i + 1) % count) for i in range(ends)]),
                cells,
                lax.ppermute(head, axis, [((i + 1) % count, i) for i in range(ends)]),
            ],
            axis=dim,
        )
    return cells


def spread(value, axis, root):
    mine = lax.axis_index(axis) == root
    return lax.psum(jnp.where(mine, value, jnp.zeros_like(value)), axis)


def elu_act(value):
    return jnp.where(value > 0, value, jnp.expm1(jnp.minimum(value, 0.0)))


def elu_slope(value):
    return jnp.where(value > 0, 1.0, jnp.exp(jnp.minimum(value, 0.0)))


def spread_acts(active, reach):
    return with_halo(active, (("seq", 0),), reach)


def spread_grads(gate, reach):
    return with_halo(gate, (("seq", 0),), reach)


def shards(saved_input, upstream, clip_lengths, conv_a, bias_a, conv_b):
    stream = saved_input[0, 0]
    lengths = clip_lengths[0]
    weights_a = conv_a[0]
    biases_a = bias_a[0]
    weights_b = conv_b[0]
    frames = stream.shape[0]
    channels = stream.shape[1]
    inner = weights_a.shape[3]
    half = KERNEL // 2
    furthest = half * 3 ** (UNITS - 1)
    offset = lax.axis_index("seq") * frames
    is_decoder = lax.axis_index("segment") == 1
    clip_ends = jnp.cumsum(lengths)
    places = offset - furthest + jnp.arange(frames + 2 * furthest, dtype=jnp.int32)
    clip_of = jnp.sum((places[:, None] >= clip_ends[None, :]).astype(jnp.int32), axis=1)
    own_clip = clip_of[furthest : furthest + frames]

    def linked(shift_by):
        return (clip_of[furthest + shift_by : furthest + shift_by + frames] == own_clip)[:, None]

    stored = []
    for unit_idx in range(UNITS):
        dilation = 3**unit_idx
        reach = half * dilation
        active = elu_act(stream.astype(jnp.float32)).astype(jnp.bfloat16)
        padded = spread_acts(active, reach)
        tap_rows = jnp.concatenate(
            [
                jnp.where(
                    linked((tap_no - half) * dilation),
                    padded[
                        reach
                        + (tap_no - half) * dilation : reach
                        + (tap_no - half) * dilation
                        + frames
                    ],
                    jnp.zeros((), jnp.bfloat16),
                )
                for tap_no in range(KERNEL)
            ],
            axis=1,
        )
        pre_act = biases_a[unit_idx][None, :] + jnp.dot(
            tap_rows,
            weights_a[unit_idx].reshape(KERNEL * channels, inner),
            preferred_element_type=jnp.float32,
        )
        squashed = elu_act(pre_act).astype(jnp.bfloat16)
        next_stream = (
            stream.astype(jnp.float32)
            + jnp.dot(squashed, weights_b[unit_idx], preferred_element_type=jnp.float32)
        ).astype(jnp.bfloat16)
        stored.append((stream, tap_rows, pre_act, squashed))
        stream = next_stream

    def unit_back(unit_idx, grad_y):
        dilation = 3**unit_idx
        reach = half * dilation
        stream_in, tap_rows, pre_act, squashed = stored[unit_idx]
        grad_b = lax.dot_general(
            grad_y,
            weights_b[unit_idx],
            (((1,), (1,)), ((), ())),
            preferred_element_type=jnp.float32,
        )
        gate = (grad_b * elu_slope(pre_act)).astype(jnp.bfloat16)
        gate_padded = spread_grads(gate, reach)
        back_rows = jnp.concatenate(
            [
                jnp.where(
                    linked(-(tap_no - half) * dilation),
                    gate_padded[
                        reach
                        - (tap_no - half) * dilation : reach
                        - (tap_no - half) * dilation
                        + frames
                    ],
                    jnp.zeros((), jnp.bfloat16),
                )
                for tap_no in range(KERNEL)
            ],
            axis=1,
        )
        turned = jnp.transpose(weights_a[unit_idx], (0, 2, 1)).reshape(KERNEL * inner, channels)
        back = jnp.dot(back_rows, turned, preferred_element_type=jnp.float32)
        grad_next = (
            grad_y.astype(jnp.float32) + back * elu_slope(stream_in.astype(jnp.float32))
        ).astype(jnp.bfloat16)
        return (gate, grad_next)

    first_gates = [None] * UNITS
    first_grads = [None] * (UNITS + 1)
    grad_y = upstream[0]
    first_grads[UNITS] = grad_y
    for unit_idx in reversed(range(UNITS)):
        gate, grad_y = unit_back(unit_idx, grad_y)
        first_gates[unit_idx] = gate
        first_grads[unit_idx] = grad_y
    latent = spread(grad_y, "segment", 1)
    grads_a = [None] * UNITS
    grads_bias = [None] * UNITS
    grads_b = [None] * UNITS
    contract = (((0,), (0,)), ((), ()))
    grad_y = latent
    for unit_idx in reversed(range(UNITS)):
        stream_in, tap_rows, pre_act, squashed = stored[unit_idx]
        gate_two, grad_next = unit_back(unit_idx, grad_y)
        gate = jnp.where(is_decoder, first_gates[unit_idx], gate_two)
        grad_out = jnp.where(is_decoder, first_grads[unit_idx + 1], grad_y)
        unit_b = lax.dot_general(squashed, grad_out, contract, preferred_element_type=jnp.float32)
        unit_bias = jnp.sum(gate.astype(jnp.float32), axis=0)
        unit_a = lax.dot_general(
            tap_rows, gate, contract, preferred_element_type=jnp.float32
        ).reshape(KERNEL, channels, inner)
        grads_a[unit_idx] = unit_a
        grads_bias[unit_idx] = unit_bias
        grads_b[unit_idx] = unit_b
        grad_y = grad_next
    section_grad = jnp.where(is_decoder, first_grads[0], grad_y)
    total_a = jnp.stack(grads_a)
    total_bias = jnp.stack(grads_bias)
    total_b = jnp.stack(grads_b)
    total_a, total_bias, total_b = lax.psum((total_a, total_bias, total_b), ("dp", "seq"))
    return (section_grad[None, None], total_a[None], total_bias[None], total_b[None])


def solution(mesh):
    placed = (
        P("segment", "dp", "seq", None),
        P("dp", "seq", None),
        P("dp", None),
        P("segment", None, None, None, None),
        P("segment", None, None),
        P("segment", None, None, None),
    )
    return jax.shard_map(
        shards,
        mesh=mesh,
        in_specs=placed,
        out_specs=(
            P("segment", "dp", "seq", None),
            P("segment", None, None, None, None),
            P("segment", None, None),
            P("segment", None, None, None),
        ),
        check_vma=False,
    )
```

profile of v0, /device:TPU:32, one launch (start us, length us, event | category | flops | bytes accessed | tf_op | source)
XLA Modules:
  0.0 530.8 jit_solution(7893162154168476364)
XLA Ops:
  8.4 3.7 collective-permute-start.1
  12.1 2.1 collective-permute-start
  15.6 3.7 slice_bitcast_fusion.2
  21.9 3.8 collective-permute-start.2
  25.7 2.0 collective-permute-start.3
  28.3 4.1 collective-permute-done.3
  34.5 3.9 collective-permute-start.4
  38.5 1.9 collective-permute-start.5
  40.9 4.3 collective-permute-done.5
  47.8 1.9 collective-permute-start.6
  49.7 2.2 copy.20
  52.0 4.1 collective-permute-start.7
  61.3 1.9 collective-permute-start.8
  63.3 2.2 copy.21
  65.5 4.1 collective-permute-start.9
  74.6 1.9 collective-permute-start.10
  77.9 4.4 collective-permute-start.11
  85.3 1.5 broadcast_select_fusion.3
  86.9 37.4 %all-reduce.4.cloned.1.call-done = bf16[512,256]{1,0:T(8,128)(2,1)} async-done(((bf16[512,256]{1,0:T(8,128)(2,1)}), bf16[512,256]{1,0:T(8,128)(2,1)}) %all-reduce.4.cloned.1.call-update) | async-done | bytes 262160 | tf_op jit(solution)/shard_map/psum | solution.py:29
  124.3 2.1 convert_reduce_fusion
  126.4 2.3 fusion.203
  128.7 3.5 collective-permute-start.13
  132.2 2.4 collective-permute-start.12
  135.0 2.8 collective-permute-done.12
  141.3 2.4 collective-permute-start.14
  144.1 3.9 collective-permute-start.15
  152.8 2.8 maximum_bitcast_fusion
  157.2 1.9 collective-permute-start.16
  159.1 349.1 %psum.30 = f32[1,3,256]{2,0,1:T(1,128)} all-reduce(f32[1,3,256]{2,0,1:T(1,128)S(1)} %broadcast_in_dim.397), channel_id=1, replica_groups=mesh['dp'=8,'seq'=16,'segment'=2] {'dp','seq'}, use_global_device_ids=true, to_apply=%region_7.8 | all-reduce | flops 768 | bytes 6144 | tf_op jit(solution)/shard_map/psum | solution.py:171
  508.2 2.0 collective-permute-start.17
  510.8 4.8 collective-permute-done.17
  517.4 5.6 %copy.80 = f32[1,3,7,256,256]{4,3,2,1,0:T(8,128)} copy(f32[1,3,7,256,256]{4,3,2,1,0:T(8,128)} %get-tuple-element.60) | data formatting | bytes 11010048
  (275 shorter events, 38.2 us)
Async XLA Ops:
  7.2 117.1 %all-reduce.4.cloned.1.call-start = ((), (), s32[]{:S(2)}) async-start(), calls=%async_computation | async-start | bytes 524288 | tf_op jit(solution)/shard_map/psum | solution.py:29
  8.4 11.6 %collective-permute-start.1 = (bf16[3,256]{1,0:T(4,128)(2,1)S(1)}, bf16[3,256]{1,0:T(4,128)(2,1)S(1)}, u32[]{:S(2)}, u32[]{:S(2)}) collective-permute-start(bf16[3,256]{1,0:T(4,128)(2,1)S(1)} %get-tuple-element.28), channel_id=1, source_target_pairs={{2,0},{4,2},{6,4},{8,6},{10,8},{12,10},{14,12},{16,14},{18,16},{20... | collective-permute-start | bytes 4616 | tf_op jit(solution)/shard_map/ppermute | solution.py:20
  12.1 7.2 %collective-permute-start = (bf16[3,256]{1,0:T(4,128)(2,1)S(1)}, bf16[3,256]{1,0:T(4,128)(2,1)S(1)}, u32[]{:S(2)}, u32[]{:S(2)}) collective-permute-start(bf16[3,256]{1,0:T(4,128)(2,1)S(1)} %get-tuple-element.29), channel_id=1, source_target_pairs={{0,2},{2,4},{4,6},{6,8},{8,10},{10,12},{12,14},{14,16},{16,18},{18... | collective-permute-start | bytes 4616 | tf_op jit(solution)/shard_map/ppermute | solution.py:18
  15.4 25.0 %copy-start.52 = (pred[512]{0:T(512)(128)(4,1)}, pred[512]{0:T(512)(128)(4,1)S(1)}, u32[]{:S(2)}) copy-start(pred[512]{0:T(512)(128)(4,1)S(1)} %get-tuple-element.43) | copy-start | bytes 1540
  15.4 30.0 %copy-start.55 = (pred[512]{0:T(512)(128)(4,1)}, pred[512]{0:T(512)(128)(4,1)S(1)}, u32[]{:S(2)}) copy-start(pred[512]{0:T(512)(128)(4,1)S(1)} %get-tuple-element.39) | copy-start | bytes 1540
  15.5 17.0 %copy-start.38 = (pred[512]{0:T(512)(128)(4,1)}, pred[512]{0:T(512)(128)(4,1)S(1)}, u32[]{:S(2)}) copy-start(pred[512]{0:T(512)(128)(4,1)S(1)} %get-tuple-element.33) | copy-start | bytes 1540
  15.5 25.0 %copy-start.41 = (pred[512]{0:T(512)(128)(4,1)}, pred[512]{0:T(512)(128)(4,1)S(1)}, u32[]{:S(2)}) copy-start(pred[512]{0:T(512)(128)(4,1)S(1)} %get-tuple-element.31) | copy-start | bytes 1540
  15.5 25.2 %copy-start.24 = (pred[512]{0:T(512)(128)(4,1)}, pred[512]{0:T(512)(128)(4,1)S(1)}, u32[]{:S(2)}) copy-start(pred[512]{0:T(512)(128)(4,1)S(1)} %get-tuple-element.35) | copy-start | bytes 1540
  15.6 29.7 %copy-start.27 = (pred[512]{0:T(512)(128)(4,1)}, pred[512]{0:T(512)(128)(4,1)S(1)}, u32[]{:S(2)}) copy-start(pred[512]{0:T(512)(128)(4,1)S(1)} %get-tuple-element.32) | copy-start | bytes 1540
  15.6 30.0 %copy-start.44 = (pred[512]{0:T(512)(128)(4,1)}, pred[512]{0:T(512)(128)(4,1)S(1)}, u32[]{:S(2)}) copy-start(pred[512]{0:T(512)(128)(4,1)S(1)} %get-tuple-element.30) | copy-start | bytes 1540
  21.9 5.9 %collective-permute-start.2 = (bf16[9,256]{1,0:T(8,128)(2,1)S(1)}, bf16[9,256]{1,0:T(8,128)(2,1)S(1)}, u32[]{:S(2)}, u32[]{:S(2)}) collective-permute-start(bf16[9,256]{1,0:T(8,128)(2,1)S(1)} %get-tuple-element.27), channel_id=1, source_target_pairs={{0,2},{2,4},{4,6},{6,8},{8,10},{10,12},{12,14},{14,16},{16,18},{18... | collective-permute-start | bytes 13832 | tf_op jit(solution)/shard_map/ppermute | solution.py:18
  25.7 6.7 %collective-permute-start.3 = (bf16[9,256]{1,0:T(8,128)(2,1)S(1)}, bf16[9,256]{1,0:T(8,128)(2,1)S(1)}, u32[]{:S(2)}, u32[]{:S(2)}) collective-permute-start(bf16[9,256]{1,0:T(8,128)(2,1)S(1)} %get-tuple-element.26), channel_id=1, source_target_pairs={{2,0},{4,2},{6,4},{8,6},{10,8},{12,10},{14,12},{16,14},{18,16},{20... | collective-permute-start | bytes 13832 | tf_op jit(solution)/shard_map/ppermute | solution.py:20
  34.5 24.4 %copy-start.18 = (f32[512,256]{1,0:T(8,128)}, f32[512,256]{1,0:T(8,128)S(1)}, u32[]{:S(2)}) copy-start(f32[512,256]{1,0:T(8,128)S(1)} %get-tuple-element.50) | copy-start | bytes 1572868
  34.5 5.9 %collective-permute-start.4 = (bf16[27,256]{1,0:T(8,128)(2,1)S(1)}, bf16[27,256]{1,0:T(8,128)(2,1)S(1)}, u32[]{:S(2)}, u32[]{:S(2)}) collective-permute-start(bf16[27,256]{1,0:T(8,128)(2,1)S(1)} %get-tuple-element.25), channel_id=1, source_target_pairs={{0,2},{2,4},{4,6},{6,8},{8,10},{10,12},{12,14},{14,16},{16,18},{18... | collective-permute-start | bytes 41480 | tf_op jit(solution)/shard_map/ppermute | solution.py:18
  38.5 6.7 %collective-permute-start.5 = (bf16[27,256]{1,0:T(8,128)(2,1)S(1)}, bf16[27,256]{1,0:T(8,128)(2,1)S(1)}, u32[]{:S(2)}, u32[]{:S(2)}) collective-permute-start(bf16[27,256]{1,0:T(8,128)(2,1)S(1)} %get-tuple-element.24), channel_id=1, source_target_pairs={{2,0},{4,2},{6,4},{8,6},{10,8},{12,10},{14,12},{16,14},{18,16},{20... | collective-permute-start | bytes 41480 | tf_op jit(solution)/shard_map/ppermute | solution.py:20
  47.8 8.2 %collective-permute-start.6 = (bf16[27,256]{1,0:T(8,128)(2,1)}, bf16[27,256]{1,0:T(8,128)(2,1)S(1)}, u32[]{:S(2)}, u32[]{:S(2)}) collective-permute-start(bf16[27,256]{1,0:T(8,128)(2,1)} %get-tuple-element.23), channel_id=1, source_target_pairs={{2,0},{4,2},{6,4},{8,6},{10,8},{12,10},{14,12},{16,14},{18,16},{20... | collective-permute-start | bytes 41480 | tf_op jit(solution)/shard_map/ppermute | solution.py:20
  52.0 6.5 %collective-permute-start.7 = (bf16[27,256]{1,0:T(8,128)(2,1)}, bf16[27,256]{1,0:T(8,128)(2,1)S(1)}, u32[]{:S(2)}, u32[]{:S(2)}) collective-permute-start(bf16[27,256]{1,0:T(8,128)(2,1)} %get-tuple-element.22), channel_id=1, source_target_pairs={{0,2},{2,4},{4,6},{6,8},{8,10},{10,12},{12,14},{14,16},{16,18},{18... | collective-permute-start | bytes 41480 | tf_op jit(solution)/shard_map/ppermute | solution.py:18
  61.3 8.3 %collective-permute-start.8 = (bf16[9,256]{1,0:T(8,128)(2,1)S(1)}, bf16[9,256]{1,0:T(8,128)(2,1)S(1)}, u32[]{:S(2)}, u32[]{:S(2)}) collective-permute-start(bf16[9,256]{1,0:T(8,128)(2,1)S(1)} %get-tuple-element.21), channel_id=1, source_target_pairs={{2,0},{4,2},{6,4},{8,6},{10,8},{12,10},{14,12},{16,14},{18,16},{20... | collective-permute-start | bytes 13832 | tf_op jit(solution)/shard_map/ppermute | solution.py:20
  65.5 5.7 %collective-permute-start.9 = (bf16[9,256]{1,0:T(8,128)(2,1)S(1)}, bf16[9,256]{1,0:T(8,128)(2,1)S(1)}, u32[]{:S(2)}, u32[]{:S(2)}) collective-permute-start(bf16[9,256]{1,0:T(8,128)(2,1)S(1)} %get-tuple-element.20), channel_id=1, source_target_pairs={{0,2},{2,4},{4,6},{6,8},{8,10},{10,12},{12,14},{14,16},{16,18},{18... | collective-permute-start | bytes 13832 | tf_op jit(solution)/shard_map/ppermute | solution.py:18
  74.6 7.7 %collective-permute-start.10 = (bf16[3,256]{1,0:T(4,128)(2,1)}, bf16[3,256]{1,0:T(4,128)(2,1)}, u32[]{:S(2)}, u32[]{:S(2)}) collective-permute-start(bf16[3,256]{1,0:T(4,128)(2,1)} %get-tuple-element.19), channel_id=1, source_target_pairs={{2,0},{4,2},{6,4},{8,6},{10,8},{12,10},{14,12},{16,14},{18,16},{20... | collective-permute-start | bytes 4616 | tf_op jit(solution)/shard_map/ppermute | solution.py:20
  77.9 6.9 %collective-permute-start.11 = (bf16[3,256]{1,0:T(4,128)(2,1)}, bf16[3,256]{1,0:T(4,128)(2,1)S(1)}, u32[]{:S(2)}, u32[]{:S(2)}) collective-permute-start(bf16[3,256]{1,0:T(4,128)(2,1)} %get-tuple-element.18), channel_id=1, source_target_pairs={{0,2},{2,4},{4,6},{6,8},{8,10},{10,12},{12,14},{14,16},{16,18},{18... | collective-permute-start | bytes 4616 | tf_op jit(solution)/shard_map/ppermute | solution.py:18
  86.8 430.6 %all-reduce.6.cloned.1.call-start = ((), (), s32[]{:S(2)}) async-start(), calls=%async_computation.1 | async-start | bytes 12582912 | tf_op jit(solution)/shard_map/psum | solution.py:171
  128.7 9.6 %collective-permute-start.13 = (bf16[27,256]{1,0:T(8,128)(2,1)S(1)}, bf16[27,256]{1,0:T(8,128)(2,1)S(1)}, u32[]{:S(2)}, u32[]{:S(2)}) collective-permute-start(bf16[27,256]{1,0:T(8,128)(2,1)S(1)} %get-tuple-element.16), channel_id=1, source_target_pairs={{0,2},{2,4},{4,6},{6,8},{8,10},{10,12},{12,14},{14,16},{16,18},{18... | collective-permute-start | bytes 41480 | tf_op jit(solution)/shard_map/ppermute | solution.py:18
  132.2 5.6 %collective-permute-start.12 = (bf16[27,256]{1,0:T(8,128)(2,1)S(1)}, bf16[27,256]{1,0:T(8,128)(2,1)S(1)}, u32[]{:S(2)}, u32[]{:S(2)}) collective-permute-start(bf16[27,256]{1,0:T(8,128)(2,1)S(1)} %get-tuple-element.17), channel_id=1, source_target_pairs={{2,0},{4,2},{6,4},{8,6},{10,8},{12,10},{14,12},{16,14},{18,16},{20... | collective-permute-start | bytes 41480 | tf_op jit(solution)/shard_map/ppermute | solution.py:20
  141.3 6.7 %collective-permute-start.14 = (bf16[9,256]{1,0:T(8,128)(2,1)S(1)}, bf16[9,256]{1,0:T(8,128)(2,1)S(1)}, u32[]{:S(2)}, u32[]{:S(2)}) collective-permute-start(bf16[9,256]{1,0:T(8,128)(2,1)S(1)} %get-tuple-element.15), channel_id=1, source_target_pairs={{2,0},{4,2},{6,4},{8,6},{10,8},{12,10},{14,12},{16,14},{18,16},{20... | collective-permute-start | bytes 13832 | tf_op jit(solution)/shard_map/ppermute | solution.py:20
  144.1 5.7 %collective-permute-start.15 = (bf16[9,256]{1,0:T(8,128)(2,1)S(1)}, bf16[9,256]{1,0:T(8,128)(2,1)S(1)}, u32[]{:S(2)}, u32[]{:S(2)}) collective-permute-start(bf16[9,256]{1,0:T(8,128)(2,1)S(1)} %get-tuple-element.14), channel_id=1, source_target_pairs={{0,2},{2,4},{4,6},{6,8},{8,10},{10,12},{12,14},{14,16},{16,18},{18... | collective-permute-start | bytes 13832 | tf_op jit(solution)/shard_map/ppermute | solution.py:18
  156.5 353.9 %copy-start.34 = (pred[512]{0:T(512)(128)(4,1)S(1)}, pred[512]{0:T(512)(128)(4,1)}, u32[]{:S(2)}) copy-start(pred[512]{0:T(512)(128)(4,1)} %copy-done.33) | copy-start | bytes 1540
  156.5 354.1 %copy-start.32 = (pred[512]{0:T(512)(128)(4,1)S(1)}, pred[512]{0:T(512)(128)(4,1)}, u32[]{:S(2)}) copy-start(pred[512]{0:T(512)(128)(4,1)} %copy-done.31) | copy-start | bytes 1540
  156.5 359.0 %copy-start.51 = (pred[512]{0:T(512)(128)(4,1)S(1)}, pred[512]{0:T(512)(128)(4,1)}, u32[]{:S(2)}) copy-start(pred[512]{0:T(512)(128)(4,1)} %copy-done.49) | copy-start | bytes 1540
  156.6 359.1 %copy-start.48 = (pred[512]{0:T(512)(128)(4,1)S(1)}, pred[512]{0:T(512)(128)(4,1)}, u32[]{:S(2)}) copy-start(pred[512]{0:T(512)(128)(4,1)} %copy-done.46) | copy-start | bytes 1540
  157.2 353.1 %collective-permute-start.16 = (bf16[3,256]{1,0:T(4,128)(2,1)S(1)}, bf16[3,256]{1,0:T(4,128)(2,1)S(1)}, u32[]{:S(2)}, u32[]{:S(2)}) collective-permute-start(bf16[3,256]{1,0:T(4,128)(2,1)S(1)} %get-tuple-element.13), channel_id=1, source_target_pairs={{2,0},{4,2},{6,4},{8,6},{10,8},{12,10},{14,12},{16,14},{18,16},{20... | collective-permute-start | bytes 4616 | tf_op jit(solution)/shard_map/ppermute | solution.py:20
  508.2 7.3 %collective-permute-start.17 = (bf16[3,256]{1,0:T(4,128)(2,1)S(1)}, bf16[3,256]{1,0:T(4,128)(2,1)S(1)}, u32[]{:S(2)}, u32[]{:S(2)}) collective-permute-start(bf16[3,256]{1,0:T(4,128)(2,1)S(1)} %get-tuple-element.12), channel_id=1, source_target_pairs={{0,2},{2,4},{4,6},{6,8},{8,10},{10,12},{12,14},{14,16},{16,18},{18... | collective-permute-start | bytes 4616 | tf_op jit(solution)/shard_map/ppermute | solution.py:18
  (63 other events, 366.4 us)
Sparse Core Ops, SparseCore 0:
  86.9 37.3 all-reduce.3
  156.7 249.6 all-reduce.5
where the time goes:
time: 532 us; the launch traced here: 531 us
  blocking collectives  349 us (66%)
  waiting for transfers between devices  55.9 us (11%)
  starting transfers between devices  51.9 us (10%)
  local copies, waits for them, and re-layouts  22.6 us (4%)
  matrix products  18.8 us (4%)
  other arithmetic  16.8 us (3%)
  between operations  15.8 us (3%)
    psum x1, blocking collectives, shards(): lax.psum((total_a, total_bias, total_b), ('dp', 'seq'))  349 us
    psum x1, waiting for transfers between devices, spread(): return lax.psum(jnp.where(mine, value, jnp.zeros_like(value)), axis)  37.4 us
    ppermute x9, starting transfers between devices, with_halo(): lax.ppermute(tail, axis, [(i, (i + 1) % count) for i in range(ends)])  31.7 us
    ppermute x9, starting transfers between devices, with_halo(): lax.ppermute(head, axis, [((i + 1) % count, i) for i in range(ends)])  20.1 us
    ppermute x9, waiting for transfers between devices, with_halo(): lax.ppermute(head, axis, [((i + 1) % count, i) for i in range(ends)])  11.2 us
    unnamed x160, local copies, waits for them, and re-layouts  11 us
  transfers between devices with their start and end apart: 20, of which 7 were waited for; matrix products, arithmetic and copies ran while one was open for 4% of the time, Pallas kernels for 0%

commit v1 on v0

--- a/solution.py
+++ b/solution.py
@@ -26,7 +26,7 @@
 
 def spread(value, axis, root):
     mine = lax.axis_index(axis) == root
-    return lax.psum(jnp.where(mine, value, jnp.zeros_like(value)), axis)
+    return jnp.sum(lax.all_gather(jnp.where(mine, value, jnp.zeros_like(value)), axis), axis=0)
 
 
 def elu_act(value):

time: 532 us -> 505 us (0.949)
  waiting for transfers between devices: 55.9 us -> 17.3 us
  blocking collectives: 349 us -> 357 us
    psum x1 -> x0, waiting for transfers between devices: 37.4 us -> none  [spread(): return lax.psum(jnp.where(mine, value, jnp.zeros_like(value)), axis)]
    psum x1, blocking collectives: 349 us -> 355 us  [shards(): lax.psum((total_a, total_bias, total_b), ('dp', 'seq'))]
  transfers between devices with their start and end apart: 20 -> 19, of which waited for: 7 -> 6; matrix products, arithmetic and copies ran while one was open for 4% -> 4% of each run, Pallas kernels for 0% -> 0%
where the time goes in v1:
time: 505 us; the launch traced here: 504 us
  blocking collectives  357 us (71%)
  starting transfers between devices  54.8 us (11%)
  local copies, waits for them, and re-layouts  22.6 us (4%)
  matrix products  18.6 us (4%)
  other arithmetic  17.6 us (3%)
  waiting for transfers between devices  17.3 us (3%)
  between operations  15.8 us (3%)
    psum x1, blocking collectives, shards(): lax.psum((total_a, total_bias, total_b), ('dp', 'seq'))  355 us
    ppermute x9, starting transfers between devices, with_halo(): lax.ppermute(tail, axis, [(i, (i + 1) % count) for i in range(ends)])  35.6 us
    ppermute x9, starting transfers between devices, with_halo(): lax.ppermute(head, axis, [((i + 1) % count, i) for i in range(ends)])  19.2 us
    unnamed x160, local copies, waits for them, and re-layouts  11 us
    unnamed x46, other arithmetic  10.2 us
  transfers between devices with their start and end apart: 19, of which 6 were waited for; matrix products, arithmetic and copies ran while one was open for 4% of the time, Pallas kernels for 0%

profile of v1, /device:TPU:32, one launch (start us, length us, event | category | flops | bytes accessed | tf_op | source)
XLA Modules:
  0.0 504.0 jit_solution(15003480549889614042)
XLA Ops:
  8.4 3.7 collective-permute-start.1
  12.1 2.1 collective-permute-start
  15.6 3.7 slice_bitcast_fusion.2
  21.9 3.8 collective-permute-start.2
  25.8 2.0 collective-permute-start.3
  28.3 4.1 collective-permute-done.3
  34.6 3.9 collective-permute-start.4
  38.5 1.9 collective-permute-start.5
  40.9 4.3 collective-permute-done.5
  47.8 1.9 collective-permute-start.6
  49.8 2.2 copy.20
  52.0 4.1 collective-permute-start.7
  61.3 1.9 collective-permute-start.8
  63.2 2.2 copy.21
  65.5 4.1 collective-permute-start.9
  74.6 1.9 collective-permute-start.10
  77.9 4.4 collective-permute-start.11
  85.2 1.4 broadcast_select_fusion.3
  86.6 2.2 all-gather
  89.6 2.1 convert_reduce_fusion
  91.7 2.3 fusion.203
  94.0 1.9 collective-permute-start.12
  96.4 5.3 %collective-permute-start.13 = (bf16[27,256]{1,0:T(8,128)(2,1)S(1)}, bf16[27,256]{1,0:T(8,128)(2,1)S(1)}, u32[]{:S(2)}, u32[]{:S(2)}) collective-permute-start(bf16[27,256]{1,0:T(8,128)(2,1)S(1)} %get-tuple-element.16), channel_id=1, source_target_pairs={{0,2},{2,4},{4,6},{6,8},{8,10},{10,12},{12,14},{14,16},{16,18},{18... | collective-permute-start | bytes 41480 | tf_op jit(solution)/shard_map/ppermute | solution.py:18
  106.1 1.9 collective-permute-start.14
  108.5 5.5 %collective-permute-start.15 = (bf16[9,256]{1,0:T(8,128)(2,1)S(1)}, bf16[9,256]{1,0:T(8,128)(2,1)S(1)}, u32[]{:S(2)}, u32[]{:S(2)}) collective-permute-start(bf16[9,256]{1,0:T(8,128)(2,1)S(1)} %get-tuple-element.14), channel_id=1, source_target_pairs={{0,2},{2,4},{4,6},{6,8},{8,10},{10,12},{12,14},{14,16},{16,18},{18... | collective-permute-start | bytes 13832 | tf_op jit(solution)/shard_map/ppermute | solution.py:18
  118.4 2.8 maximum_bitcast_fusion
  122.8 1.9 collective-permute-start.16
  124.7 355.1 %psum.22 = f32[1,3,256]{2,0,1:T(1,128)} all-reduce(f32[1,3,256]{2,0,1:T(1,128)S(1)} %broadcast_in_dim.397), channel_id=1, replica_groups=mesh['dp'=8,'seq'=16,'segment'=2] {'dp','seq'}, use_global_device_ids=true, to_apply=%region_7.8 | all-reduce | flops 768 | bytes 6144 | tf_op jit(solution)/shard_map/psum | solution.py:171
  479.9 2.5 collective-permute-start.17
  482.9 5.9 %collective-permute-done.17 = bf16[3,256]{1,0:T(4,128)(2,1)S(1)} collective-permute-done((bf16[3,256]{1,0:T(4,128)(2,1)S(1)}, bf16[3,256]{1,0:T(4,128)(2,1)S(1)}, u32[]{:S(2)}, u32[]{:S(2)}) %collective-permute-start.17) | collective-permute-done | bytes 1568 | tf_op jit(solution)/shard_map/ppermute | solution.py:18
  489.2 1.4 fusion.23
  490.6 5.6 %copy.79 = f32[1,3,7,256,256]{4,3,2,1,0:T(8,128)} copy(f32[1,3,7,256,256]{4,3,2,1,0:T(8,128)} %get-tuple-element.60) | data formatting | bytes 11010048
  (274 shorter events, 38.0 us)
Async XLA Ops:
  7.2 483.4 %all-reduce.3.cloned.1.call-start = ((), (), s32[]{:S(2)}) async-start(), calls=%async_computation | async-start | bytes 12582912 | tf_op jit(solution)/shard_map/psum | solution.py:171
  8.4 11.6 %collective-permute-start.1 = (bf16[3,256]{1,0:T(4,128)(2,1)S(1)}, bf16[3,256]{1,0:T(4,128)(2,1)S(1)}, u32[]{:S(2)}, u32[]{:S(2)}) collective-permute-start(bf16[3,256]{1,0:T(4,128)(2,1)S(1)} %get-tuple-element.28), channel_id=1, source_target_pairs={{2,0},{4,2},{6,4},{8,6},{10,8},{12,10},{14,12},{16,14},{18,16},{20... | collective-permute-start | bytes 4616 | tf_op jit(solution)/shard_map/ppermute | solution.py:20
  12.1 7.2 %collective-permute-start = (bf16[3,256]{1,0:T(4,128)(2,1)S(1)}, bf16[3,256]{1,0:T(4,128)(2,1)S(1)}, u32[]{:S(2)}, u32[]{:S(2)}) collective-permute-start(bf16[3,256]{1,0:T(4,128)(2,1)S(1)} %get-tuple-element.29), channel_id=1, source_target_pairs={{0,2},{2,4},{4,6},{6,8},{8,10},{10,12},{12,14},{14,16},{16,18},{18... | collective-permute-start | bytes 4616 | tf_op jit(solution)/shard_map/ppermute | solution.py:18
  15.4 25.1 %copy-start.53 = (pred[512]{0:T(512)(128)(4,1)}, pred[512]{0:T(512)(128)(4,1)S(1)}, u32[]{:S(2)}) copy-start(pred[512]{0:T(512)(128)(4,1)S(1)} %get-tuple-element.43) | copy-start | bytes 1540
  15.4 30.0 %copy-start.56 = (pred[512]{0:T(512)(128)(4,1)}, pred[512]{0:T(512)(128)(4,1)S(1)}, u32[]{:S(2)}) copy-start(pred[512]{0:T(512)(128)(4,1)S(1)} %get-tuple-element.39) | copy-start | bytes 1540
  15.5 16.9 %copy-start.23 = (pred[512]{0:T(512)(128)(4,1)}, pred[512]{0:T(512)(128)(4,1)S(1)}, u32[]{:S(2)}) copy-start(pred[512]{0:T(512)(128)(4,1)S(1)} %get-tuple-element.36) | copy-start | bytes 1540
  15.5 17.0 %copy-start.39 = (pred[512]{0:T(512)(128)(4,1)}, pred[512]{0:T(512)(128)(4,1)S(1)}, u32[]{:S(2)}) copy-start(pred[512]{0:T(512)(128)(4,1)S(1)} %get-tuple-element.33) | copy-start | bytes 1540
  15.5 25.1 %copy-start.42 = (pred[512]{0:T(512)(128)(4,1)}, pred[512]{0:T(512)(128)(4,1)S(1)}, u32[]{:S(2)}) copy-start(pred[512]{0:T(512)(128)(4,1)S(1)} %get-tuple-element.31) | copy-start | bytes 1540
  15.5 25.2 %copy-start.25 = (pred[512]{0:T(512)(128)(4,1)}, pred[512]{0:T(512)(128)(4,1)S(1)}, u32[]{:S(2)}) copy-start(pred[512]{0:T(512)(128)(4,1)S(1)} %get-tuple-element.35) | copy-start | bytes 1540
  15.6 29.7 %copy-start.28 = (pred[512]{0:T(512)(128)(4,1)}, pred[512]{0:T(512)(128)(4,1)S(1)}, u32[]{:S(2)}) copy-start(pred[512]{0:T(512)(128)(4,1)S(1)} %get-tuple-element.32) | copy-start | bytes 1540
  15.6 30.0 %copy-start.45 = (pred[512]{0:T(512)(128)(4,1)}, pred[512]{0:T(512)(128)(4,1)S(1)}, u32[]{:S(2)}) copy-start(pred[512]{0:T(512)(128)(4,1)S(1)} %get-tuple-element.30) | copy-start | bytes 1540
  21.9 5.9 %collective-permute-start.2 = (bf16[9,256]{1,0:T(8,128)(2,1)S(1)}, bf16[9,256]{1,0:T(8,128)(2,1)S(1)}, u32[]{:S(2)}, u32[]{:S(2)}) collective-permute-start(bf16[9,256]{1,0:T(8,128)(2,1)S(1)} %get-tuple-element.27), channel_id=1, source_target_pairs={{0,2},{2,4},{4,6},{6,8},{8,10},{10,12},{12,14},{14,16},{16,18},{18... | collective-permute-start | bytes 13832 | tf_op jit(solution)/shard_map/ppermute | solution.py:18
  25.8 6.7 %collective-permute-start.3 = (bf16[9,256]{1,0:T(8,128)(2,1)S(1)}, bf16[9,256]{1,0:T(8,128)(2,1)S(1)}, u32[]{:S(2)}, u32[]{:S(2)}) collective-permute-start(bf16[9,256]{1,0:T(8,128)(2,1)S(1)} %get-tuple-element.26), channel_id=1, source_target_pairs={{2,0},{4,2},{6,4},{8,6},{10,8},{12,10},{14,12},{16,14},{18,16},{20... | collective-permute-start | bytes 13832 | tf_op jit(solution)/shard_map/ppermute | solution.py:20
  34.5 24.3 %copy-start.18 = (f32[512,256]{1,0:T(8,128)}, f32[512,256]{1,0:T(8,128)S(1)}, u32[]{:S(2)}) copy-start(f32[512,256]{1,0:T(8,128)S(1)} %get-tuple-element.50) | copy-start | bytes 1572868
  34.6 5.9 %collective-permute-start.4 = (bf16[27,256]{1,0:T(8,128)(2,1)S(1)}, bf16[27,256]{1,0:T(8,128)(2,1)S(1)}, u32[]{:S(2)}, u32[]{:S(2)}) collective-permute-start(bf16[27,256]{1,0:T(8,128)(2,1)S(1)} %get-tuple-element.25), channel_id=1, source_target_pairs={{0,2},{2,4},{4,6},{6,8},{8,10},{10,12},{12,14},{14,16},{16,18},{18... | collective-permute-start | bytes 41480 | tf_op jit(solution)/shard_map/ppermute | solution.py:18
  38.5 6.7 %collective-permute-start.5 = (bf16[27,256]{1,0:T(8,128)(2,1)S(1)}, bf16[27,256]{1,0:T(8,128)(2,1)S(1)}, u32[]{:S(2)}, u32[]{:S(2)}) collective-permute-start(bf16[27,256]{1,0:T(8,128)(2,1)S(1)} %get-tuple-element.24), channel_id=1, source_target_pairs={{2,0},{4,2},{6,4},{8,6},{10,8},{12,10},{14,12},{16,14},{18,16},{20... | collective-permute-start | bytes 41480 | tf_op jit(solution)/shard_map/ppermute | solution.py:20
  47.8 8.2 %collective-permute-start.6 = (bf16[27,256]{1,0:T(8,128)(2,1)}, bf16[27,256]{1,0:T(8,128)(2,1)S(1)}, u32[]{:S(2)}, u32[]{:S(2)}) collective-permute-start(bf16[27,256]{1,0:T(8,128)(2,1)} %get-tuple-element.23), channel_id=1, source_target_pairs={{2,0},{4,2},{6,4},{8,6},{10,8},{12,10},{14,12},{16,14},{18,16},{20... | collective-permute-start | bytes 41480 | tf_op jit(solution)/shard_map/ppermute | solution.py:20
  52.0 6.4 %collective-permute-start.7 = (bf16[27,256]{1,0:T(8,128)(2,1)}, bf16[27,256]{1,0:T(8,128)(2,1)S(1)}, u32[]{:S(2)}, u32[]{:S(2)}) collective-permute-start(bf16[27,256]{1,0:T(8,128)(2,1)} %get-tuple-element.22), channel_id=1, source_target_pairs={{0,2},{2,4},{4,6},{6,8},{8,10},{10,12},{12,14},{14,16},{16,18},{18... | collective-permute-start | bytes 41480 | tf_op jit(solution)/shard_map/ppermute | solution.py:18
  61.3 8.3 %collective-permute-start.8 = (bf16[9,256]{1,0:T(8,128)(2,1)S(1)}, bf16[9,256]{1,0:T(8,128)(2,1)S(1)}, u32[]{:S(2)}, u32[]{:S(2)}) collective-permute-start(bf16[9,256]{1,0:T(8,128)(2,1)S(1)} %get-tuple-element.21), channel_id=1, source_target_pairs={{2,0},{4,2},{6,4},{8,6},{10,8},{12,10},{14,12},{16,14},{18,16},{20... | collective-permute-start | bytes 13832 | tf_op jit(solution)/shard_map/ppermute | solution.py:20
  65.5 5.7 %collective-permute-start.9 = (bf16[9,256]{1,0:T(8,128)(2,1)S(1)}, bf16[9,256]{1,0:T(8,128)(2,1)S(1)}, u32[]{:S(2)}, u32[]{:S(2)}) collective-permute-start(bf16[9,256]{1,0:T(8,128)(2,1)S(1)} %get-tuple-element.20), channel_id=1, source_target_pairs={{0,2},{2,4},{4,6},{6,8},{8,10},{10,12},{12,14},{14,16},{16,18},{18... | collective-permute-start | bytes 13832 | tf_op jit(solution)/shard_map/ppermute | solution.py:18
  74.6 7.7 %collective-permute-start.10 = (bf16[3,256]{1,0:T(4,128)(2,1)}, bf16[3,256]{1,0:T(4,128)(2,1)}, u32[]{:S(2)}, u32[]{:S(2)}) collective-permute-start(bf16[3,256]{1,0:T(4,128)(2,1)} %get-tuple-element.19), channel_id=1, source_target_pairs={{2,0},{4,2},{6,4},{8,6},{10,8},{12,10},{14,12},{16,14},{18,16},{20... | collective-permute-start | bytes 4616 | tf_op jit(solution)/shard_map/ppermute | solution.py:20
  77.9 6.9 %collective-permute-start.11 = (bf16[3,256]{1,0:T(4,128)(2,1)}, bf16[3,256]{1,0:T(4,128)(2,1)S(1)}, u32[]{:S(2)}, u32[]{:S(2)}) collective-permute-start(bf16[3,256]{1,0:T(4,128)(2,1)} %get-tuple-element.18), channel_id=1, source_target_pairs={{0,2},{2,4},{4,6},{6,8},{8,10},{10,12},{12,14},{14,16},{16,18},{18... | collective-permute-start | bytes 4616 | tf_op jit(solution)/shard_map/ppermute | solution.py:18
  94.0 7.7 %collective-permute-start.12 = (bf16[27,256]{1,0:T(8,128)(2,1)S(1)}, bf16[27,256]{1,0:T(8,128)(2,1)S(1)}, u32[]{:S(2)}, u32[]{:S(2)}) collective-permute-start(bf16[27,256]{1,0:T(8,128)(2,1)S(1)} %get-tuple-element.17), channel_id=1, source_target_pairs={{2,0},{4,2},{6,4},{8,6},{10,8},{12,10},{14,12},{16,14},{18,16},{20... | collective-permute-start | bytes 41480 | tf_op jit(solution)/shard_map/ppermute | solution.py:20
  96.4 6.7 %collective-permute-start.13 = (bf16[27,256]{1,0:T(8,128)(2,1)S(1)}, bf16[27,256]{1,0:T(8,128)(2,1)S(1)}, u32[]{:S(2)}, u32[]{:S(2)}) collective-permute-start(bf16[27,256]{1,0:T(8,128)(2,1)S(1)} %get-tuple-element.16), channel_id=1, source_target_pairs={{0,2},{2,4},{4,6},{6,8},{8,10},{10,12},{12,14},{14,16},{16,18},{18... | collective-permute-start | bytes 41480 | tf_op jit(solution)/shard_map/ppermute | solution.py:18
  106.1 7.9 %collective-permute-start.14 = (bf16[9,256]{1,0:T(8,128)(2,1)S(1)}, bf16[9,256]{1,0:T(8,128)(2,1)S(1)}, u32[]{:S(2)}, u32[]{:S(2)}) collective-permute-start(bf16[9,256]{1,0:T(8,128)(2,1)S(1)} %get-tuple-element.15), channel_id=1, source_target_pairs={{2,0},{4,2},{6,4},{8,6},{10,8},{12,10},{14,12},{16,14},{18,16},{20... | collective-permute-start | bytes 13832 | tf_op jit(solution)/shard_map/ppermute | solution.py:20
  108.5 6.9 %collective-permute-start.15 = (bf16[9,256]{1,0:T(8,128)(2,1)S(1)}, bf16[9,256]{1,0:T(8,128)(2,1)S(1)}, u32[]{:S(2)}, u32[]{:S(2)}) collective-permute-start(bf16[9,256]{1,0:T(8,128)(2,1)S(1)} %get-tuple-element.14), channel_id=1, source_target_pairs={{0,2},{2,4},{4,6},{6,8},{8,10},{10,12},{12,14},{14,16},{16,18},{18... | collective-permute-start | bytes 13832 | tf_op jit(solution)/shard_map/ppermute | solution.py:18
  122.1 360.4 %copy-start.35 = (pred[512]{0:T(512)(128)(4,1)S(1)}, pred[512]{0:T(512)(128)(4,1)}, u32[]{:S(2)}) copy-start(pred[512]{0:T(512)(128)(4,1)} %copy-done.34) | copy-start | bytes 1540
  122.1 360.6 %copy-start.33 = (pred[512]{0:T(512)(128)(4,1)S(1)}, pred[512]{0:T(512)(128)(4,1)}, u32[]{:S(2)}) copy-start(pred[512]{0:T(512)(128)(4,1)} %copy-done.32) | copy-start | bytes 1540
  122.1 366.6 %copy-start.52 = (pred[512]{0:T(512)(128)(4,1)S(1)}, pred[512]{0:T(512)(128)(4,1)}, u32[]{:S(2)}) copy-start(pred[512]{0:T(512)(128)(4,1)} %copy-done.50) | copy-start | bytes 1540
  122.1 366.7 %copy-start.49 = (pred[512]{0:T(512)(128)(4,1)S(1)}, pred[512]{0:T(512)(128)(4,1)}, u32[]{:S(2)}) copy-start(pred[512]{0:T(512)(128)(4,1)} %copy-done.47) | copy-start | bytes 1540
  122.8 359.6 %collective-permute-start.16 = (bf16[3,256]{1,0:T(4,128)(2,1)S(1)}, bf16[3,256]{1,0:T(4,128)(2,1)S(1)}, u32[]{:S(2)}, u32[]{:S(2)}) collective-permute-start(bf16[3,256]{1,0:T(4,128)(2,1)S(1)} %get-tuple-element.13), channel_id=1, source_target_pairs={{2,0},{4,2},{6,4},{8,6},{10,8},{12,10},{14,12},{16,14},{18,16},{20... | collective-permute-start | bytes 4616 | tf_op jit(solution)/shard_map/ppermute | solution.py:20
  479.9 8.8 %collective-permute-start.17 = (bf16[3,256]{1,0:T(4,128)(2,1)S(1)}, bf16[3,256]{1,0:T(4,128)(2,1)S(1)}, u32[]{:S(2)}, u32[]{:S(2)}) collective-permute-start(bf16[3,256]{1,0:T(4,128)(2,1)S(1)} %get-tuple-element.12), channel_id=1, source_target_pairs={{0,2},{2,4},{4,6},{6,8},{8,10},{10,12},{12,14},{14,16},{16,18},{18... | collective-permute-start | bytes 4616 | tf_op jit(solution)/shard_map/ppermute | solution.py:18
  (62 other events, 354.6 us)
Sparse Core Ops, SparseCore 0:
  122.3 255.6 all-reduce.2
